TPU v7x, 256 devices: a whole 4x4x8 slice. The times are simulated.
256 devices in a mesh: dp: 8 (over x, core), expert: 32 (over y, z).
Axes of the slice: x: 4, y: 4, z: 8, core: 2. Of those that a mesh axis runs over, the one named last changes fastest.
Arguments:
- tokens: bfloat16 [8192, 2048], P(('dp', 'expert')), may hold values from -6 to 6
- expert_ids: int32 [8192, 8], P(('dp', 'expert')), may hold values from 0 to 31, all different within a row; in each aligned block of 32 rows (0 to 31, 32 to 63, ...) at most 16 rows name the same one
- gate_weights: float32 [8192, 8], P(('dp', 'expert')), may hold values from 0.05 to 0.35
- grad_output: bfloat16 [8192, 2048], P(('dp', 'expert')), may hold values from -6 to 6
- w_gate_up: bfloat16 [32, 2048, 1536], P('expert'), may hold values from -0.125 to 0.125
- w_down: bfloat16 [32, 768, 2048], P('expert'), may hold values from -0.21875 to 0.21875
Outputs:
- mixed: bfloat16 [8192, 2048], P(('dp', 'expert'))
- grad_tokens: bfloat16 [8192, 2048], P(('dp', 'expert'))
- grad_gates: float32 [8192, 8], P(('dp', 'expert'))
- grad_gate_up: float32 [32, 2048, 1536], P('expert', 'dp')
- grad_down: float32 [32, 768, 2048], P('expert', None, 'dp')
Inputs may be any that keep to these rules, and one draw needn't show every extreme that they name: `expert_ids`: in each block of 32 rows (the rows of one device) every expert is named at most 16 times, a bound that some block reaches; a row names 8 different experts, and every expert is named somewhere.
All inputs are finite; a program needn't handle non-finite values.
Results may differ from a plain program's by a relative error of at most 0.015.
Values may be sent and summed in bfloat16 or wider, within the bound.
No kernel may reach another device: no remote copies, remote signals or barrier semaphores. Data moves between devices by JAX's collectives and lax.ppermute only.
A program may use at most 128 MiB of HBM per device.

v0:
```python
import jax
import jax.numpy as jnp
from jax import lax
from jax.sharding import PartitionSpec as P


def swish_parts(gate_up, hidden_units):
    gate_half = gate_up[..., :hidden_units]
    up_half = gate_up[..., hidden_units:]
    sigmoid_part = jax.nn.sigmoid(gate_half)
    return (gate_half, up_half, sigmoid_part)


def body(tokens, expert_ids, gate_weights, grad_output, w_gate_up, w_down):
    token_count, top_count = expert_ids.shape
    width = tokens.shape[1]
    per_device = w_gate_up.shape[0]
    hidden_units = w_down.shape[1]
    owners = lax.axis_size("expert")
    expert_total = owners * per_device
    capacity = min(token_count, 2 * token_count * top_count // expert_total)
    pair_count = token_count * top_count
    me = lax.axis_index("expert")
    all_tokens = lax.all_gather(tokens, "expert", tiled=True).reshape(owners, token_count, width)
    all_ids = lax.all_gather(expert_ids, "expert", tiled=True).reshape(owners, pair_count)
    all_gates = lax.all_gather(gate_weights, "expert", tiled=True).reshape(owners, pair_count)
    all_grad = lax.all_gather(grad_output, "expert", tiled=True).reshape(owners, token_count, width)
    local_experts = me * per_device + jnp.arange(per_device, dtype=jnp.int32)
    onehot = all_ids[:, :, None] == local_experts[None, None, :]
    onehot_i = onehot.astype(jnp.int32)
    slots = jnp.cumsum(onehot_i, axis=1) - onehot_i
    slot_axis = jnp.arange(capacity, dtype=jnp.int32)
    sel = jnp.logical_and(onehot[..., None], slots[..., None] == slot_axis).transpose(2, 0, 3, 1)
    sel_f = sel.astype(jnp.float32)
    row_gate = jnp.sum(sel_f * all_gates[None, :, None, :], axis=3)
    sel_tok = jnp.sum(
        sel.reshape(per_device, owners, capacity, token_count, top_count).astype(jnp.bfloat16),
        axis=4,
    )
    x_rows = jnp.einsum(
        "jsct,std->jscd", sel_tok, all_tokens, preferred_element_type=jnp.float32
    ).astype(jnp.bfloat16)
    dy_rows = jnp.einsum("jsct,std->jscd", sel_tok, all_grad, preferred_element_type=jnp.float32)
    x_rows = x_rows.reshape(per_device, owners * capacity, width)
    dy_rows = dy_rows.reshape(per_device, owners * capacity, width)
    row_gate = row_gate.reshape(per_device, owners * capacity)
    gate_up = jnp.einsum("jrd,jdf->jrf", x_rows, w_gate_up, preferred_element_type=jnp.float32)
    gate_half, up_half, sigmoid_part = swish_parts(gate_up, hidden_units)
    swish = gate_half * sigmoid_part
    hidden = (swish * up_half).astype(jnp.bfloat16)
    out_rows = jnp.einsum(
        "jrf,jfd->jrd", hidden, w_down, preferred_element_type=jnp.float32
    ).astype(jnp.bfloat16)
    grad_rows = (row_gate[..., None] * dy_rows).astype(jnp.bfloat16)
    grad_hidden = jnp.einsum("jrd,jfd->jrf", grad_rows, w_down, preferred_element_type=jnp.float32)
    grad_gate = grad_hidden * up_half * sigmoid_part * (1.0 + gate_half * (1.0 - sigmoid_part))
    grad_up = grad_hidden * swish
    grad_act = jnp.concatenate([grad_gate, grad_up], axis=2).astype(jnp.bfloat16)
    grad_in = jnp.einsum(
        "jrf,jdf->jrd", grad_act, w_gate_up, preferred_element_type=jnp.float32
    ).astype(jnp.bfloat16)
    out_f = out_rows.astype(jnp.float32)
    row_inner = jnp.sum(out_f * dy_rows, axis=2).reshape(per_device, owners, capacity)
    gate_part = jnp.sum(sel_f * row_inner[..., None], axis=(0, 2)).reshape(
        owners * token_count, top_count
    )
    weighted = (row_gate[..., None] * out_f).astype(jnp.bfloat16)
    mixed_part = jnp.einsum(
        "jsct,jscd->std",
        sel_tok,
        weighted.reshape(per_device, owners, capacity, width),
        preferred_element_type=jnp.float32,
    ).astype(jnp.bfloat16)
    mixed = lax.psum_scatter(
        mixed_part.reshape(owners * token_count, width), "expert", scatter_dimension=0, tiled=True
    )
    grad_gates = lax.psum_scatter(gate_part, "expert", scatter_dimension=0, tiled=True)
    tokens_part = jnp.einsum(
        "jsct,jscd->std",
        sel_tok,
        grad_in.reshape(per_device, owners, capacity, width),
        preferred_element_type=jnp.float32,
    ).astype(jnp.bfloat16)
    grad_tokens = lax.psum_scatter(
        tokens_part.reshape(owners * token_count, width), "expert", scatter_dimension=0, tiled=True
    )
    down_local = jnp.einsum("jrf,jrd->jfd", hidden, grad_rows, preferred_element_type=jnp.float32)
    gate_up_local = jnp.einsum("jrd,jrf->jdf", x_rows, grad_act, preferred_element_type=jnp.float32)
    grad_gate_up = lax.psum_scatter(
        gate_up_local.astype(jnp.bfloat16), "dp", scatter_dimension=1, tiled=True
    ).astype(jnp.float32)
    grad_down = lax.psum_scatter(
        down_local.astype(jnp.bfloat16), "dp", scatter_dimension=2, tiled=True
    ).astype(jnp.float32)
    return (mixed, grad_tokens, grad_gates, grad_gate_up, grad_down)


def solution(mesh):
    in_specs = (
        P(("dp", "expert"), None),
        P(("dp", "expert"), None),
        P(("dp", "expert"), None),
        P(("dp", "expert"), None),
        P("expert", None, None),
        P("expert", None, None),
    )
    out_specs = (
        P(("dp", "expert"), None),
        P(("dp", "expert"), None),
        P(("dp", "expert"), None),
        P("expert", "dp", None),
        P("expert", None, "dp"),
    )
    return jax.shard_map(body, mesh=mesh, in_specs=in_specs, out_specs=out_specs, check_vma=False)
```

profile of v0, /device:TPU:2, one launch (start us, length us, event | category | flops | bytes accessed | tf_op | source)
XLA Modules:
  0.0 953.2 jit_solution(4402269293742463482)
XLA Ops:
  8.7 46.8 %all-gather = s32[32,32,8]{1,2,0:T(8,128)S(1)} all-gather(s32[1,32,8]{1,2,0:T(8,128)} %bitcast.123), channel_id=1, replica_groups=mesh['dp'=8,'expert'=32] {'expert'}, dimensions={0}, use_global_device_ids=true | all-gather | bytes 33792 | tf_op jit(solution)/shard_map/all_gather | solution.py:25
  59.8 42.4 %all-gather.1 = f32[32,32,8]{1,2,0:T(8,128)S(1)} all-gather(f32[1,32,8]{1,2,0:T(8,128)S(1)} %bitcast.124), channel_id=1, replica_groups=mesh['dp'=8,'expert'=32] {'expert'}, dimensions={0}, use_global_device_ids=true | all-gather | bytes 33792 | tf_op jit(solution)/shard_map/all_gather | solution.py:26
  103.0 4.3 convolution_convert_fusion.4
  107.3 69.6 %all-gather.7.cloned.1.call-done = bf16[1024,2048]{1,0:T(8,128)(2,1)} async-done(((bf16[32,2048]{1,0:T(8,128)(2,1)}), bf16[1024,2048]{1,0:T(8,128)(2,1)}) %all-gather.7.cloned.1.call-update) | async-done | bytes 4194320 | tf_op jit(solution)/shard_map/all_gather | solution.py:27
  176.8 3.0 fusion.44
  179.9 7.1 fusion.7
  187.5 3.2 fusion.6
  190.8 1.6 select_reduce_fusion
  192.7 1.1 reshape.312
  193.9 6.0 fusion.20
  200.1 5.5 fusion.33
  206.7 5.5 fusion
  212.3 2.0 fusion.5
  214.3 3.3 convolution_convert_fusion.2
  217.7 6.7 fusion.17
  224.5 3.4 convolution_convert_fusion.1
  227.9 179.2 %reduce-scatter.10.cloned.1.call-done = f32[32,8]{1,0:T(8,128)} async-done(((f32[1024,8]{1,0:T(8,128)}), f32[32,8]{1,0:T(8,128)}) %reduce-scatter.10.cloned.1.call-update) | async-done | bytes 1040 | tf_op jit(solution)/shard_map/reduce_scatter | solution.py:77
  407.1 1.4 copy.33
  408.4 34.5 %reduce-scatter.14.cloned.1.call-done = bf16[1,768,256]{2,1,0:T(8,128)(2,1)} async-done(((bf16[1,768,2048]{2,1,0:T(8,128)(2,1)}), bf16[1,768,256]{2,1,0:T(8,128)(2,1)}) %reduce-scatter.14.cloned.1.call-update) | async-done | bytes 393232 | tf_op jit(solution)/shard_map/reduce_scatter | solution.py:92
  443.0 1.9 convert_element_type.155
  444.9 45.7 %reduce-scatter.12.cloned.1.call-done = bf16[1,256,1536]{2,1,0:T(8,128)(2,1)} async-done(((bf16[1,2048,1536]{2,1,0:T(8,128)(2,1)}), bf16[1,256,1536]{2,1,0:T(8,128)(2,1)}) %reduce-scatter.12.cloned.1.call-update) | async-done | bytes 786448 | tf_op jit(solution)/shard_map/reduce_scatter | solution.py:89
  490.6 2.5 convert_element_type.152
  493.1 227.1 %reduce-scatter.6.cloned.1.call-done = bf16[32,2048]{1,0:T(8,128)(2,1)} async-done(((bf16[1024,2048]{1,0:T(8,128)(2,1)}), bf16[32,2048]{1,0:T(8,128)(2,1)}) %reduce-scatter.6.cloned.1.call-update) | async-done | bytes 131088 | tf_op jit(solution)/shard_map/reduce_scatter | solution.py:74
  720.2 226.1 %reduce-scatter.8.cloned.1.call-done = bf16[32,2048]{1,0:T(8,128)(2,1)} async-done(((bf16[1024,2048]{1,0:T(8,128)(2,1)}), bf16[32,2048]{1,0:T(8,128)(2,1)}) %reduce-scatter.8.cloned.1.call-update) | async-done | bytes 131088 | tf_op jit(solution)/shard_map/reduce_scatter | solution.py:84
  (54 shorter events, 8.9 us)
Async XLA Ops:
  7.2 180.3 %copy-start = (bf16[1,768,2048]{2,1,0:T(8,128)(2,1)S(1)}, bf16[1,768,2048]{2,1,0:T(8,128)(2,1)}, u32[]{:S(2)}) copy-start(bf16[1,768,2048]{2,1,0:T(8,128)(2,1)} %param.11) | copy-start | bytes 9437188
  7.2 52.6 %copy-start.7 = (f32[32,8]{0,1:T(8,128)S(1)}, f32[32,8]{0,1:T(8,128)}, u32[]{:S(2)}) copy-start(f32[32,8]{0,1:T(8,128)} %param.8) | copy-start | bytes 3076
  7.2 95.8 %all-gather.5.cloned.1.call-start = ((), (), s32[]{:S(2)}) async-start(), calls=%async_computation.5 | async-start | bytes 4325376 | tf_op jit(solution)/shard_map/all_gather | solution.py:24
  7.9 168.9 %all-gather.7.cloned.1.call-start = ((), (), s32[]{:S(2)}) async-start(), calls=%async_computation.7 | async-start | bytes 4325376 | tf_op jit(solution)/shard_map/all_gather | solution.py:27
  8.7 398.4 %reduce-scatter.10.cloned.1.call-start = ((), (), s32[]{:S(2)}) async-start(), calls=%async_computation.9 | async-start | bytes 540672 | tf_op jit(solution)/shard_map/reduce_scatter | solution.py:77
  58.2 0.6 copy-start.6
  176.8 3.0 copy-start.4
  179.9 7.6 copy-start.1
  186.9 3.7 copy-start.2
  187.5 3.2 copy-start.3
  193.8 249.1 %reduce-scatter.14.cloned.1.call-start = ((), (), s32[]{:S(2)}) async-start(), calls=%async_computation.11 | async-start | bytes 3538944 | tf_op jit(solution)/shard_map/reduce_scatter | solution.py:92
  199.8 290.8 %reduce-scatter.12.cloned.1.call-start = ((), (), s32[]{:S(2)}) async-start(), calls=%async_computation.10 | async-start | bytes 7077888 | tf_op jit(solution)/shard_map/reduce_scatter | solution.py:89
  200.1 6.6 copy-start.5
  205.6 0.9 copy-start.8
  205.6 1.1 copy-start.9
  212.3 507.9 %reduce-scatter.6.cloned.1.call-start = ((), (), s32[]{:S(2)}) async-start(), calls=%async_computation.6 | async-start | bytes 4325376 | tf_op jit(solution)/shard_map/reduce_scatter | solution.py:74
  217.7 728.6 %reduce-scatter.8.cloned.1.call-start = ((), (), s32[]{:S(2)}) async-start(), calls=%async_computation.8 | async-start | bytes 4325376 | tf_op jit(solution)/shard_map/reduce_scatter | solution.py:84
Sparse Core Ops, SparseCore 0:
  10.6 84.9 all-gather.4
  98.2 78.5 all-gather.6
  193.9 213.0 reduce-scatter.9
  409.5 33.4 reduce-scatter.13
  445.4 45.2 reduce-scatter.11
  494.9 225.2 reduce-scatter.5
  724.7 221.5 reduce-scatter.7
where the time goes:
time: 954 us; the launch traced here: 953 us
  waiting for transfers between devices  784 us (82%)
  blocking collectives  89.2 us (9%)
  matrix products  47.9 us (5%)
  between operations  14.3 us (1%)
  other arithmetic  10.6 us (1%)
    reduce_scatter x1, waiting for transfers between devices, body(): lax.psum_scatter(mixed_part.reshape(owners * token_count, width), 'expert...  227 us
    reduce_scatter x1, waiting for transfers between devices, body(): lax.psum_scatter(tokens_part.reshape(owners * token_count, width), 'exper...  226 us
    reduce_scatter x1, waiting for transfers between devices, body(): lax.psum_scatter(gate_part, 'expert', scatter_dimension=0, tiled=True)  179 us
    all_gather x1, waiting for transfers between devices, body(): lax.all_gather(grad_output, 'expert', tiled=True)  69.6 us
    all_gather x1, blocking collectives, body(): lax.all_gather(expert_ids, 'expert', tiled=True).reshape(owners, pair_count)  46.8 us
    reduce_scatter x1, waiting for transfers between devices, body(): lax.psum_scatter(gate_up_local.astype(jnp.bfloat16), 'dp', scatter_dimens...  45.7 us
    all_gather x1, blocking collectives, body(): lax.all_gather(gate_weights, 'expert', tiled=True)  42.4 us
    reduce_scatter x1, waiting for transfers between devices, body(): lax.psum_scatter(down_local.astype(jnp.bfloat16), 'dp', scatter_dimension...  34.5 us
  transfers between devices with their start and end apart: 7, of which 6 were waited for; matrix products, arithmetic and copies ran while one was open for 5% of the time, Pallas kernels for 0%

commit v1 on v0

--- a/solution.py
+++ b/solution.py
@@ -24,7 +24,12 @@
     all_tokens = lax.all_gather(tokens, "expert", tiled=True).reshape(owners, token_count, width)
     all_ids = lax.all_gather(expert_ids, "expert", tiled=True).reshape(owners, pair_count)
     all_gates = lax.all_gather(gate_weights, "expert", tiled=True).reshape(owners, pair_count)
-    all_grad = lax.all_gather(grad_output, "expert", tiled=True).reshape(owners, token_count, width)
+    all_grad = jnp.concatenate(
+        lax.all_to_all(
+            jnp.stack([grad_output for _ in range(lax.axis_size("expert"))], axis=0), "expert", 0, 0
+        ),
+        0,
+    ).reshape(owners, token_count, width)
     local_experts = me * per_device + jnp.arange(per_device, dtype=jnp.int32)
     onehot = all_ids[:, :, None] == local_experts[None, None, :]
     onehot_i = onehot.astype(jnp.int32)

time: 954 us -> 1010 us (1.059)
  blocking collectives: 89.2 us -> 194 us
  waiting for transfers between devices: 784 us -> 715 us
  starting transfers between devices: 0.46 us -> 12.2 us
    all_gather x1, blocking collectives: 46.8 us -> 152 us  [body(): lax.all_gather(expert_ids, 'expert', tiled=True).reshape(owners, pair_count)]
    all_gather x1 -> x0, waiting for transfers between devices: 69.6 us -> none  [body(): lax.all_gather(grad_output, 'expert', tiled=True)]
    all_to_all x0 -> x1, starting transfers between devices: none -> 11.7 us  [body(): lax.all_to_all(jnp.stack([grad_output for _ in range(lax.axis_size('exper...]
  transfers between devices with their start and end apart: 7 -> 7, of which waited for: 6 -> 5; matrix products, arithmetic and copies ran while one was open for 5% -> 6% of each run, Pallas kernels for 0% -> 0%
where the time goes in v1:
time: 1010 us; the launch traced here: 1000 us
  waiting for transfers between devices  715 us (71%)
  blocking collectives  194 us (19%)
  matrix products  45.7 us (5%)
  between operations  14.3 us (1%)
  local copies, waits for them, and re-layouts  12.3 us (1%)
  starting transfers between devices  12.2 us (1%)
  other arithmetic  11.5 us (1%)
    reduce_scatter x1, waiting for transfers between devices, body(): lax.psum_scatter(mixed_part.reshape(owners * token_count, width), 'expert...  227 us
    reduce_scatter x1, waiting for transfers between devices, body(): lax.psum_scatter(tokens_part.reshape(owners * token_count, width), 'exper...  226 us
    reduce_scatter x1, waiting for transfers between devices, body(): lax.psum_scatter(gate_part, 'expert', scatter_dimension=0, tiled=True)  180 us
    all_gather x1, blocking collectives, body(): lax.all_gather(expert_ids, 'expert', tiled=True).reshape(owners, pair_count)  152 us
    reduce_scatter x1, waiting for transfers between devices, body(): lax.psum_scatter(gate_up_local.astype(jnp.bfloat16), 'dp', scatter_dimens...  45.8 us
    all_gather x1, blocking collectives, body(): lax.all_gather(gate_weights, 'expert', tiled=True)  41.8 us
    reduce_scatter x1, waiting for transfers between devices, body(): lax.psum_scatter(down_local.astype(jnp.bfloat16), 'dp', scatter_dimension...  34.6 us
  transfers between devices with their start and end apart: 7, of which 5 were waited for; matrix products, arithmetic and copies ran while one was open for 6% of the time, Pallas kernels for 0%

profile of v1, /device:TPU:2, one launch (start us, length us, event | category | flops | bytes accessed | tf_op | source)
XLA Modules:
  0.0 1004.9 jit_solution(17495335565019682165)
XLA Ops:
  7.9 3.6 stack.2
  11.5 11.7 %all-to-all-start = ((bf16[32,32,2048]{2,1,0:T(8,128)(2,1)}), bf16[32,32,2048]{2,1,0:T(8,128)(2,1)}, u32[]{:S(2)}, u32[]{:S(2)}) async-start(bf16[32,32,2048]{2,1,0:T(8,128)(2,1)} %stack.2), calls=%async_computation.1 | async-start | bytes 8388608 | tf_op jit(solution)/shard_map/all_to_all | solution.py:28
  23.3 152.4 %all-gather = s32[32,32,8]{1,2,0:T(8,128)S(1)} all-gather(s32[1,32,8]{1,2,0:T(8,128)S(1)} %bitcast.121), channel_id=1, replica_groups=mesh['dp'=8,'expert'=32] {'expert'}, dimensions={0}, use_global_device_ids=true | all-gather | bytes 33792 | tf_op jit(solution)/shard_map/all_gather | solution.py:25
  180.0 41.8 %all-gather.1 = f32[32,32,8]{1,2,0:T(8,128)S(1)} all-gather(f32[1,32,8]{1,2,0:T(8,128)S(1)} %bitcast.122), channel_id=1, replica_groups=mesh['dp'=8,'expert'=32] {'expert'}, dimensions={0}, use_global_device_ids=true | all-gather | bytes 33792 | tf_op jit(solution)/shard_map/all_gather | solution.py:26
  222.6 2.9 convolution_convert_fusion.4
  225.5 6.3 fusion.7
  231.9 1.7 copy-done.2
  235.0 2.9 fusion.44
  237.9 3.2 fusion.6
  241.3 1.6 select_reduce_fusion
  244.4 6.0 fusion.20
  250.6 5.5 fusion.33
  257.2 5.5 fusion
  262.8 2.0 fusion.5
  264.8 3.3 convolution_convert_fusion.2
  268.2 6.7 fusion.17
  275.0 3.4 convolution_convert_fusion.1
  278.4 180.3 %reduce-scatter.10.cloned.1.call-done = f32[32,8]{1,0:T(8,128)} async-done(((f32[1024,8]{1,0:T(8,128)}), f32[32,8]{1,0:T(8,128)}) %reduce-scatter.10.cloned.1.call-update) | async-done | bytes 1040 | tf_op jit(solution)/shard_map/reduce_scatter | solution.py:82
  460.0 34.6 %reduce-scatter.14.cloned.1.call-done = bf16[1,768,256]{2,1,0:T(8,128)(2,1)} async-done(((bf16[1,768,2048]{2,1,0:T(8,128)(2,1)}), bf16[1,768,256]{2,1,0:T(8,128)(2,1)}) %reduce-scatter.14.cloned.1.call-update) | async-done | bytes 393232 | tf_op jit(solution)/shard_map/reduce_scatter | solution.py:97
  494.6 1.9 convert_element_type.155
  496.5 45.8 %reduce-scatter.12.cloned.1.call-done = bf16[1,256,1536]{2,1,0:T(8,128)(2,1)} async-done(((bf16[1,2048,1536]{2,1,0:T(8,128)(2,1)}), bf16[1,256,1536]{2,1,0:T(8,128)(2,1)}) %reduce-scatter.12.cloned.1.call-update) | async-done | bytes 786448 | tf_op jit(solution)/shard_map/reduce_scatter | solution.py:94
  542.3 2.5 convert_element_type.152
  544.8 227.2 %reduce-scatter.6.cloned.1.call-done = bf16[32,2048]{1,0:T(8,128)(2,1)} async-done(((bf16[1024,2048]{1,0:T(8,128)(2,1)}), bf16[32,2048]{1,0:T(8,128)(2,1)}) %reduce-scatter.6.cloned.1.call-update) | async-done | bytes 131088 | tf_op jit(solution)/shard_map/reduce_scatter | solution.py:79
  772.0 226.0 %reduce-scatter.8.cloned.1.call-done = bf16[32,2048]{1,0:T(8,128)(2,1)} async-done(((bf16[1024,2048]{1,0:T(8,128)(2,1)}), bf16[32,2048]{1,0:T(8,128)(2,1)}) %reduce-scatter.8.cloned.1.call-update) | async-done | bytes 131088 | tf_op jit(solution)/shard_map/reduce_scatter | solution.py:89
  (56 shorter events, 11.6 us)
Async XLA Ops:
  7.2 230.7 %copy-start = (bf16[1,768,2048]{2,1,0:T(8,128)(2,1)S(1)}, bf16[1,768,2048]{2,1,0:T(8,128)(2,1)}, u32[]{:S(2)}) copy-start(bf16[1,768,2048]{2,1,0:T(8,128)(2,1)} %param.11) | copy-start | bytes 9437188
  7.2 215.5 %all-gather.4.cloned.1.call-start = ((), (), s32[]{:S(2)}) async-start(), calls=%async_computation.6 | async-start | bytes 4325376 | tf_op jit(solution)/shard_map/all_gather | solution.py:24
  11.5 11.8 %copy-start.7 = (s32[32,8]{0,1:T(8,128)S(1)}, s32[32,8]{0,1:T(8,128)}, u32[]{:S(2)}) copy-start(s32[32,8]{0,1:T(8,128)} %param.7) | copy-start | bytes 3076
  11.5 168.5 %copy-start.8 = (f32[32,8]{0,1:T(8,128)S(1)}, f32[32,8]{0,1:T(8,128)}, u32[]{:S(2)}) copy-start(f32[32,8]{0,1:T(8,128)} %param.8) | copy-start | bytes 3076
  11.5 223.4 %all-to-all-start = ((bf16[32,32,2048]{2,1,0:T(8,128)(2,1)}), bf16[32,32,2048]{2,1,0:T(8,128)(2,1)}, u32[]{:S(2)}, u32[]{:S(2)}) async-start(bf16[32,32,2048]{2,1,0:T(8,128)(2,1)} %stack.2), calls=%async_computation.1 | async-start | bytes 8388608 | tf_op jit(solution)/shard_map/all_to_all | solution.py:28
  23.3 435.4 %reduce-scatter.10.cloned.1.call-start = ((), (), s32[]{:S(2)}) async-start(), calls=%async_computation.9 | async-start | bytes 540672 | tf_op jit(solution)/shard_map/reduce_scatter | solution.py:82
  178.4 0.6 copy-start.6
  225.5 6.3 copy-start.4
  231.8 1.8 copy-start.2
  235.0 3.0 copy-start.3
  237.9 3.2 copy-start.1
  244.3 250.3 %reduce-scatter.14.cloned.1.call-start = ((), (), s32[]{:S(2)}) async-start(), calls=%async_computation.11 | async-start | bytes 3538944 | tf_op jit(solution)/shard_map/reduce_scatter | solution.py:97
  250.4 291.9 %reduce-scatter.12.cloned.1.call-start = ((), (), s32[]{:S(2)}) async-start(), calls=%async_computation.10 | async-start | bytes 7077888 | tf_op jit(solution)/shard_map/reduce_scatter | solution.py:94
  250.6 6.6 copy-start.5
  256.1 0.9 copy-start.9
  256.1 1.1 copy-start.10
  262.8 509.2 %reduce-scatter.6.cloned.1.call-start = ((), (), s32[]{:S(2)}) async-start(), calls=%async_computation.7 | async-start | bytes 4325376 | tf_op jit(solution)/shard_map/reduce_scatter | solution.py:79
  268.2 729.8 %reduce-scatter.8.cloned.1.call-start = ((), (), s32[]{:S(2)}) async-start(), calls=%async_computation.8 | async-start | bytes 4325376 | tf_op jit(solution)/shard_map/reduce_scatter | solution.py:89
Sparse Core Ops, SparseCore 0:
  10.6 130.9 all-gather.3
  244.5 214.1 reduce-scatter.9
  461.2 33.3 reduce-scatter.13
  497.0 45.2 reduce-scatter.11
  546.6 225.3 reduce-scatter.5
  776.3 221.6 reduce-scatter.7
